TPU v7x, 256 devices: a whole 4x4x8 slice. The times are simulated.
256 devices in a mesh: dp: 8 (over y_lo, x), space: 32 (over y_hi, z, core).
Axes of the slice: x: 4, y: 4 (y_hi: 2, y_lo: 2; y = y_hi * 2 + y_lo), z: 8, core: 2. Of those that a mesh axis runs over, the one named last changes fastest.
Arguments:
- images: bfloat16 [8, 256, 64, 1536], P('dp', 'space'), may hold values from -8 to 8
- dw_kernel: bfloat16 [7, 7, 1536], replicated, may hold values from -0.875 to 0.875
- dw_bias: float32 [1536], replicated, may hold values from -3 to 3
- ln_gain: float32 [1536], replicated, may hold values from 0.1 to 1.9
- ln_shift: float32 [1536], replicated, may hold values from -2 to 2
- proj: bfloat16 [1536, 1024], replicated, may hold values from -0.15625 to 0.15625
- text: float32 [8, 1024], P('dp'), may hold values from -6 to 6
- logit_scale: float32 [1], replicated, may hold values from 10 to 100
Outputs:
- loss: float32 [], replicated
- grad_images: bfloat16 [8, 256, 64, 1536], P('dp', 'space')
- kernel_grad: float32 [7, 7, 1536], replicated
- text_grad: float32 [8, 1024], P('dp')
All inputs are finite; a program needn't handle non-finite values.
Results may differ from a plain program's by a relative error of at most 0.0013.
Values may be sent and summed in bfloat16 or wider, within the bound.
No kernel may reach another device: no remote copies, remote signals or barrier semaphores. Data moves between devices by JAX's collectives and lax.ppermute only.
A program may use at most 128 MiB of HBM per device.

v0:
```python
import jax
import jax.numpy as jnp
from jax import lax
from jax.sharding import PartitionSpec as P


def with_halo(block, sides, width):
    for axis, dim in sides:
        count = lax.axis_size(axis)
        forward = [(i, i + 1) for i in range(count - 1)]
        backward = [(target, source) for source, target in forward]
        low = lax.ppermute(
            lax.slice_in_dim(block, block.shape[dim] - width, None, axis=dim), axis, forward
        )
        high = lax.ppermute(lax.slice_in_dim(block, 0, width, axis=dim), axis, backward)
        block = jnp.concatenate([low, block, high], axis=dim)
    return block


def normalize(values):
    centre_value = jnp.mean(values, axis=-1, keepdims=True)
    centred = values - centre_value
    spread = jnp.mean(centred * centred, axis=-1, keepdims=True)
    inv_dev = lax.rsqrt(spread + 1e-06)
    return (centred * inv_dev, inv_dev)


def convolve(padded, kernel_float, row_count, col_count):
    result = None
    for a in range(kernel_float.shape[0]):
        for d in range(kernel_float.shape[1]):
            product = padded[:, a : a + row_count, d : d + col_count, :] * kernel_float[a, d]
            result = product if result is None else result + product
    return result


def logsum(scores, axis):
    highest = jnp.max(scores, axis=axis, keepdims=True)
    return jnp.squeeze(highest, axis) + jnp.log(jnp.sum(jnp.exp(scores - highest), axis=axis))


def shards(images, dw_kernel, dw_bias, ln_gain, ln_shift, proj, text, logit_scale):
    batch_dev, row_count, col_count, channels = images.shape
    height = row_count * lax.axis_size("space")
    pixel_count = height * col_count
    reach_rows = dw_kernel.shape[0] // 2
    kernel_float = dw_kernel.astype(jnp.float32)
    extended = with_halo(images, (("space", 1),), reach_rows)
    padded_all = jnp.pad(
        extended.astype(jnp.float32), ((0, 0), (0, 0), (reach_rows, reach_rows), (0, 0))
    )
    conv_out = convolve(padded_all, kernel_float, row_count, col_count) + dw_bias
    normed, inv_dev = normalize(conv_out)
    pool_part = jnp.sum(normed * ln_gain + ln_shift, axis=(1, 2))
    proj_float = proj.astype(jnp.float32)
    pooled = lax.psum(pool_part, "space") / pixel_count
    embedded = jnp.dot(pooled, proj_float, precision=lax.Precision.HIGHEST)
    emb_norm = jnp.sqrt(jnp.sum(embedded * embedded, axis=-1, keepdims=True))
    unit_img = embedded / emb_norm
    text_norm = jnp.sqrt(jnp.sum(text * text, axis=-1, keepdims=True))
    unit_txt = text / text_norm
    all_img, all_txt = (
        lax.all_gather(unit_img, "dp", axis=0, tiled=True),
        lax.all_gather(unit_txt, "dp", axis=0, tiled=True),
    )
    factor = logit_scale[0]
    row_scores = factor * jnp.dot(unit_img, all_txt.T, precision=lax.Precision.HIGHEST)
    col_scores = factor * jnp.dot(all_img, unit_txt.T, precision=lax.Precision.HIGHEST)
    row_logsum = logsum(row_scores, 1)
    col_logsum = logsum(col_scores, 0)
    batch_count = all_img.shape[0]
    owned = lax.axis_index("dp") * batch_dev + jnp.arange(batch_dev, dtype=jnp.int32)
    identity_rows = (jnp.arange(batch_count, dtype=jnp.int32)[None, :] == owned[:, None]).astype(
        jnp.float32
    )
    diagonal = jnp.sum(row_scores * identity_rows, axis=1)
    all_row_logsum, all_col_logsum = (
        lax.all_gather(row_logsum, "dp", axis=0, tiled=True),
        lax.all_gather(col_logsum, "dp", axis=0, tiled=True),
    )
    local_terms = jnp.sum(row_logsum - diagonal) + jnp.sum(col_logsum - diagonal)
    loss = lax.psum(local_terms, "dp") / (2 * batch_count)
    row_grad = (
        0.5
        * (
            jnp.exp(row_scores - row_logsum[:, None])
            + jnp.exp(row_scores - all_col_logsum[None, :])
        )
        - identity_rows
    )
    col_grad = (
        0.5
        * (
            jnp.exp(col_scores - all_row_logsum[:, None])
            + jnp.exp(col_scores - col_logsum[None, :])
        )
        - identity_rows.T
    )
    unit_img_grad = factor * jnp.dot(row_grad, all_txt, precision=lax.Precision.HIGHEST)
    unit_txt_grad = factor * jnp.dot(col_grad.T, all_img, precision=lax.Precision.HIGHEST)
    text_grad = (
        unit_txt_grad - unit_txt * jnp.sum(unit_txt * unit_txt_grad, axis=-1, keepdims=True)
    ) / text_norm
    emb_grad = (
        unit_img_grad - unit_img * jnp.sum(unit_img * unit_img_grad, axis=-1, keepdims=True)
    ) / emb_norm
    weighted = jnp.dot(emb_grad, proj_float.T, precision=lax.Precision.HIGHEST) * ln_gain
    weight_rows = weighted[:, None, None, :]
    weight_mean = jnp.mean(weighted, axis=-1)[:, None, None, None]
    spread_term = jnp.mean(weight_rows * normed, axis=-1, keepdims=True)
    grad_own = inv_dev * (weight_rows - weight_mean - normed * spread_term)
    grad_wide = with_halo(grad_own, (("space", 1),), reach_rows)
    grad_pad = jnp.pad(grad_wide, ((0, 0), (0, 0), (reach_rows, reach_rows), (0, 0)))
    input_grad = None
    for a in range(kernel_float.shape[0]):
        for d in range(kernel_float.shape[1]):
            start_row = 2 * reach_rows - a
            start_col = 2 * reach_rows - d
            product = (
                kernel_float[a, d]
                * grad_pad[
                    :, start_row : start_row + row_count, start_col : start_col + col_count, :
                ]
            )
            input_grad = product if input_grad is None else input_grad + product
    kernel_part = jnp.stack(
        [
            jnp.stack(
                [
                    jnp.sum(
                        grad_own * padded_all[:, a : a + row_count, d : d + col_count, :],
                        axis=(0, 1, 2),
                    )
                    for d in range(kernel_float.shape[1])
                ]
            )
            for a in range(kernel_float.shape[0])
        ]
    )
    kernel_grad = lax.psum(kernel_part, ("dp", "space")) / pixel_count
    return (loss, input_grad.astype(jnp.bfloat16), kernel_grad, text_grad)


def solution(mesh):
    placed = (P("dp", "space", None, None), P(), P(), P(), P(), P(), P("dp", None), P())
    return jax.shard_map(
        shards,
        mesh=mesh,
        in_specs=placed,
        out_specs=(P(), P("dp", "space", None, None), P(), P("dp", None)),
        check_vma=False,
    )
```

profile of v0, /device:TPU:1, one launch (start us, length us, event | category | flops | bytes accessed | tf_op | source)
XLA Modules:
  0.0 721.8 jit_solution(10826175399687109468)
XLA Ops:
  7.2 2.5 fusion.104
  9.7 4.9 collective-permute-start
  14.6 2.3 collective-permute-start.1
  17.6 1.3 multiply_reduce_fusion.53
  19.6 0.9 convert_element_type.28
  20.6 1.3 dynamic-slice
  22.5 22.0 %all-gather.1 = f32[8,1,1024]{2,1,0:T(1,128)S(1)} all-gather(f32[1,1,1024]{2,1,0:T(1,128)S(1)} %fusion.113), channel_id=1, replica_groups=mesh['dp'=8,'space'=32] {'dp'}, dimensions={0}, use_global_device_ids=true | all-gather | bytes 36864 | tf_op jit(solution)/shard_map/all_gather | solution.py:64
  45.3 0.9 slice_reduce_fusion.48
  46.3 4.5 maximum_convert_fusion
  51.2 72.7 %fusion.102 = (f32[8,64]{1,0:T(8,128)S(1)}, f32[1,8,64,1536]{3,2,1,0:T(8,128)}) fusion(f32[1536]{0:T(1024)S(1)} %copy-done.86, f32[1536]{0:T(1024)S(1)} %get-tuple-element.54, f32[1536]{0:T(1024)S(1)} %get-tuple-element.55, f32[1536]{0:T(1024)S(1)} %get-tuple-element.56, f32[1536]{0:T(1024)S(1)} %get-tuple-element.57, ...), kind=kLoop, calls=%fused_computation.331 | loop fusion | flops 77856256 | bytes 30996480 | tf_op jit(solution)/shard_map/reduce_sum | solution.py:21
  123.9 2.5 multiply_reduce_fusion.50
  127.3 74.9 %psum.21 = f32[1,1536]{1,0:T(1,128)S(1)} all-reduce(f32[1,1536]{1,0:T(1,128)S(1)} %reduce_sum.564), channel_id=1, replica_groups=mesh['dp'=8,'space'=32] {'space'}, use_global_device_ids=true, to_apply=%region_3.4 | all-reduce | flops 1536 | bytes 12288 | tf_op jit(solution)/shard_map/psum | solution.py:56
  202.2 1.3 fusion.67
  204.9 21.9 %all-gather = f32[8192]{0:T(1024)S(1)} all-gather(f32[1024]{0:T(1024)S(1)} %broadcast_divide_fusion.1), channel_id=2, replica_groups=mesh['dp'=8,'space'=32] {'dp'}, dimensions={0}, use_global_device_ids=true | all-gather | bytes 36864 | tf_op jit(solution)/shard_map/all_gather | solution.py:63
  227.6 1.3 fusion.79
  231.0 1.2 exponential_reduce_fusion
  236.2 16.2 %all-reduce.4 = (f32[]{:T(128)}, f32[8]{0:T(128)S(1)}, f32[8]{0:T(128)S(1)}) all-reduce(f32[]{:T(128)} %bitcast.11, f32[8]{0:T(128)S(1)} %dynamic-update-slice, f32[8]{0:T(128)S(1)} %dynamic-update-slice.1), channel_id=1, replica_groups=mesh['dp'=8,'space'=32] {'dp'}, use_global_device_ids=true, to_apply=%region_11.12 | all-reduce | flops 17 | bytes 136 | tf_op jit(solution)/shard_map/psum | solution.py:82
  253.4 1.2 subtract_divide_fusion.1
  254.7 2.5 convolution_reduce_fusion
  259.1 30.2 %multiply_reduce_fusion = (f32[1536]{0:T(1024)S(1)}, f32[1536]{0:T(1024)S(1)}, f32[1536]{0:T(1024)S(1)}, f32[1536]{0:T(1024)S(1)}, f32[1536]{0:T(1024)S(1)}, /*i...) fusion(f32[1,14,64,1536]{3,2,1,0:T(8,128)} %maximum_convert_fus, ...), kind=kLoop, calls=%fused_computation.157 | loop fusion | flops 32216064 | bytes 21356544 | tf_op jit(solution)/shard_map/reduce_sum | solution.py:130
  289.3 22.3 %multiply_reduce_fusion.36 = (f32[1536]{0:T(1024)S(1)}, f32[1536]{0:T(1024)S(1)}, f32[1536]{0:T(1024)S(1)}, f32[1536]{0:T(1024)S(1)}, f32[1536]{0:T(1024)S(1)}, ...) fusion(f32[1,8,64,1536]{3,2,1,0:T(8,128)S(1)} %get-tuple-elemen, ...), kind=kLoop, calls=%fused_computation.193 | loop fusion | flops 20427264 | bytes 15022080 | tf_op jit(solution)/shard_map/reduce_sum | solution.py:130
  311.6 27.4 %multiply_reduce_fusion.1 = (f32[1536]{0:T(1024)S(1)}, f32[1536]{0:T(1024)S(1)}, f32[1536]{0:T(1024)S(1)}, f32[1536]{0:T(1024)S(1)}, f32[1536]{0:T(1024)S(1)}, /...) fusion(f32[1,8,64,1536]{3,2,1,0:T(8,128)S(1)} %get-tuple-elemen, ...), kind=kLoop, calls=%fused_computation.158 | loop fusion | flops 28283904 | bytes 15052800 | tf_op jit(solution)/shard_map/reduce_sum | solution.py:130
  339.1 1.5 fusion.103
  365.8 7.9 %collective-permute-start.2 = (f32[1,3,64,1536]{3,2,1,0:T(8,128)}, f32[1,3,64,1536]{3,2,1,0:T(8,128)}, u32[]{:S(2)}, u32[]{:S(2)}) collective-permute-start(f32[1,3,64,1536]{3,2,1,0:T(8,128)} %get-tuple-element.112), channel_id=1, source_target_pairs={{0,1},{1,2},{2,3},{3,4},{4,5},{5,6},{6,7},{7,8},{8,9},{9,10},{10,1... | collective-permute-start | bytes 3538952 | tf_op jit(solution)/shard_map/ppermute | solution.py:12
  373.8 6.8 collective-permute-start.3
  383.2 0.9 stack.235
  387.1 1.4 multiply_reduce_fusion.51
  388.5 1.9 subtract_divide_fusion
  390.4 245.9 %all-reduce.7.cloned.1.call-done = f32[7,7,1536]{2,1,0:T(8,128)} async-done(((f32[7,7,1536]{2,1,0:T(8,128)}), f32[7,7,1536]{2,1,0:T(8,128)}) %all-reduce.7.cloned.1.call-update) | async-done | bytes 301072 | tf_op jit(solution)/shard_map/psum | solution.py:140
  636.3 1.7 broadcast_multiply_fusion
  638.5 4.7 select_maximum_fusion
  643.6 70.2 %fusion.59 = bf16[1,8,64,1536]{3,2,1,0:T(8,128)(2,1)} fusion(f32[1,14,70,1536]{3,2,1,0:T(8,128)} %select_maximum_fusion, f32[1,8,64,1536]{3,2,1,0:T(8,128)} %copy-done.1, f32[1,3,64,1536]{3,2,1,0:T(8,128)} %collective-permute-done.2, f32[1,3,64,1536]{3,2,1,0:T(8,128)} %collective-permute-done.3, f32[1536]{0:T(1024)S(1)} %copy-done.64, ...), kind=kLoop, calls=%fused_computation.211 | loop fusion | flops 81788928 | bytes 139499520 | tf_op jit(solution)/shard_map/convert_element_type | solution.py:141
  (265 shorter events, 38.5 us)
Async XLA Ops:
  7.2 195.1 %copy-start = (bf16[1536,1024]{1,0:T(8,128)(2,1)S(1)}, bf16[1536,1024]{1,0:T(8,128)(2,1)}, u32[]{:S(2)}) copy-start(bf16[1536,1024]{1,0:T(8,128)(2,1)} %param.13) | copy-start | bytes 9437188
  7.2 629.2 %all-reduce.7.cloned.1.call-start = ((), (), s32[]{:S(2)}) async-start(), calls=%async_computation | async-start | bytes 688128 | tf_op jit(solution)/shard_map/psum | solution.py:140
  9.7 36.6 %collective-permute-start = (bf16[1,3,64,1536]{3,2,1,0:T(8,128)(2,1)}, bf16[1,3,64,1536]{3,2,1,0:T(8,128)(2,1)}, u32[]{:S(2)}, u32[]{:S(2)}) collective-permute-start(bf16[1,3,64,1536]{3,2,1,0:T(8,128)(2,1)} %get-tuple-element.114), channel_id=1, source_target_pairs={{0,1},{1,2},{2,3},{3,4},{4,5},{5,6},{6,7},{7,8},{8,9},{9,10},{10,1... | collective-permute-start | bytes 1769480 | tf_op jit(solution)/shard_map/ppermute | solution.py:12
  14.6 31.6 %collective-permute-start.1 = (bf16[1,3,64,1536]{3,2,1,0:T(8,128)(2,1)}, bf16[1,3,64,1536]{3,2,1,0:T(8,128)(2,1)}, u32[]{:S(2)}, u32[]{:S(2)}) collective-permute-start(bf16[1,3,64,1536]{3,2,1,0:T(8,128)(2,1)} %get-tuple-element.115), channel_id=1, source_target_pairs={{1,0},{2,1},{3,2},{4,3},{5,4},{6,5},{7,6},{8,7},{9,8},{10,9},{11,1... | collective-permute-start | bytes 1769480 | tf_op jit(solution)/shard_map/ppermute | solution.py:15
  44.7 6.1 copy-start.5
  44.7 6.1 copy-start.7
  44.7 6.1 copy-start.9
  44.7 6.1 copy-start.11
  44.7 6.1 copy-start.13
  44.7 6.1 copy-start.15
  44.7 6.1 copy-start.17
  44.7 6.1 copy-start.19
  44.8 6.1 copy-start.21
  45.1 5.8 copy-start.23
  45.1 5.8 copy-start.25
  45.1 5.8 copy-start.27
  45.1 5.8 copy-start.29
  45.1 5.8 copy-start.31
  45.1 5.8 copy-start.33
  45.2 5.8 copy-start.35
  45.2 5.8 copy-start.37
  45.2 5.8 copy-start.39
  45.2 5.8 copy-start.41
  45.2 5.8 copy-start.43
  45.2 5.8 copy-start.45
  45.2 5.8 copy-start.47
  45.2 5.8 copy-start.49
  45.2 5.8 copy-start.51
  126.7 103.5 %copy-start.83 = (f32[1,1024]{1,0:T(1,128)S(1)}, f32[1,1024]{1,0:T(1,128)}, u32[]{:S(2)}) copy-start(f32[1,1024]{1,0:T(1,128)} %param.14) | copy-start | bytes 12292
  289.3 49.7 %copy-start.1 = (f32[1,8,64,1536]{3,2,1,0:T(8,128)}, f32[1,8,64,1536]{3,2,1,0:T(8,128)S(1)}, u32[]{:S(2)}) copy-start(f32[1,8,64,1536]{3,2,1,0:T(8,128)S(1)} %get-tuple-element.107) | copy-start | bytes 9437188
  365.8 272.6 %collective-permute-start.2 = (f32[1,3,64,1536]{3,2,1,0:T(8,128)}, f32[1,3,64,1536]{3,2,1,0:T(8,128)}, u32[]{:S(2)}, u32[]{:S(2)}) collective-permute-start(f32[1,3,64,1536]{3,2,1,0:T(8,128)} %get-tuple-element.112), channel_id=1, source_target_pairs={{0,1},{1,2},{2,3},{3,4},{4,5},{5,6},{6,7},{7,8},{8,9},{9,10},{10,1... | collective-permute-start | bytes 3538952 | tf_op jit(solution)/shard_map/ppermute | solution.py:12
  373.8 264.7 %collective-permute-start.3 = (f32[1,3,64,1536]{3,2,1,0:T(8,128)}, f32[1,3,64,1536]{3,2,1,0:T(8,128)}, u32[]{:S(2)}, u32[]{:S(2)}) collective-permute-start(f32[1,3,64,1536]{3,2,1,0:T(8,128)} %get-tuple-element.113), channel_id=1, source_target_pairs={{1,0},{2,1},{3,2},{4,3},{5,4},{6,5},{7,6},{8,7},{9,8},{10,9},{11,1... | collective-permute-start | bytes 3538952 | tf_op jit(solution)/shard_map/ppermute | solution.py:15
  (60 other events, 296.8 us)
Sparse Core Ops, SparseCore 0:
  386.7 249.6 all-reduce.6
where the time goes:
time: 723 us; the launch traced here: 722 us
  other arithmetic  249 us (34%)
  waiting for transfers between devices  246 us (34%)
  blocking collectives  135 us (19%)
  local copies, waits for them, and re-layouts  40 us (6%)
  between operations  23.8 us (3%)
  starting transfers between devices  22 us (3%)
    psum x1, waiting for transfers between devices, shards(): kernel_grad = lax.psum(kernel_part, ('dp', 'space')) / pixel_count  246 us
    reduce_sum x3, other arithmetic, shards(): jnp.sum(grad_own * padded_all[:, a:a + row_count, d:d + col_count, :], ax...  80 us
    psum x1, blocking collectives, shards(): pooled = lax.psum(pool_part, 'space') / pixel_count  74.9 us
    reduce_sum x1, other arithmetic, normalize(): centre_value = jnp.mean(values, axis=-1, keepdims=True)  72.7 us
    convert_element_type x1, other arithmetic, shards(): return (loss, input_grad.astype(jnp.bfloat16), kernel_grad, text_grad)  70.2 us
    another operation x56, local copies, waits for them, and re-layouts, shards(): jnp.stack([jnp.sum(grad_own * padded_all[:, a:a + row_count, d:d + col_co...  30.3 us
    all_gather x1, blocking collectives, shards(): lax.all_gather(unit_txt, 'dp', axis=0, tiled=True)  22 us
    all_gather x1, blocking collectives, shards(): lax.all_gather(unit_img, 'dp', axis=0, tiled=True)  21.9 us
  transfers between devices with their start and end apart: 5, of which 1 were waited for; matrix products, arithmetic and copies ran while one was open for 2% of the time, Pallas kernels for 0%

commit v1 on v0

--- a/solution.py
+++ b/solution.py
@@ -137,7 +137,7 @@
             for a in range(kernel_float.shape[0])
         ]
     )
-    kernel_grad = lax.psum(kernel_part, ("dp", "space")) / pixel_count
+    kernel_grad = jnp.sum(lax.all_gather(kernel_part, ("dp", "space")), axis=0) / pixel_count
     return (loss, input_grad.astype(jnp.bfloat16), kernel_grad, text_grad)
 
 

time: 723 us -> 968 us (1.34)
  waiting for transfers between devices: 246 us -> 426 us
  local copies, waits for them, and re-layouts: 40 us -> 72.1 us
  other arithmetic: 249 us -> 280 us
    all_gather x0 -> x1, waiting for transfers between devices: none -> 397 us  [shards(): lax.all_gather(kernel_part, ('dp', 'space'))]
    psum x1 -> x0, waiting for transfers between devices: 246 us -> none  [shards(): kernel_grad = lax.psum(kernel_part, ('dp', 'space')) / pixel_count]
    another operation x56, local copies, waits for them, and re-layouts: 30.3 us -> 59.6 us  [shards(): jnp.stack([jnp.sum(grad_own * padded_all[:, a:a + row_count, d:d + col_co...]
    reduce_sum x0 -> x1, other arithmetic: none -> 27.1 us  [shards(): jnp.sum(lax.all_gather(kernel_part, ('dp', 'space')), axis=0) / pixel_count]
    ppermute x2, waiting for transfers between devices: 0.01 us -> 16.2 us  [with_halo(): lax.ppermute(lax.slice_in_dim(block, 0, width, axis=dim), axis, backward)]
    ppermute x2, waiting for transfers between devices: 0.01 us -> 12.1 us  [with_halo(): lax.ppermute(lax.slice_in_dim(block, block.shape[dim] - width, None, axis...]
  transfers between devices with their start and end apart: 5 -> 5, of which waited for: 1 -> 3; matrix products, arithmetic and copies ran while one was open for 2% -> 9% of each run, Pallas kernels for 0% -> 0%
where the time goes in v1:
time: 968 us; the launch traced here: 964 us
  waiting for transfers between devices  426 us (44%)
  other arithmetic  280 us (29%)
  blocking collectives  135 us (14%)
  local copies, waits for them, and re-layouts  72.1 us (7%)
  between operations  23.8 us (2%)
  starting transfers between devices  21.4 us (2%)
    all_gather x1, waiting for transfers between devices, shards(): lax.all_gather(kernel_part, ('dp', 'space'))  397 us
    reduce_sum x3, other arithmetic, shards(): jnp.sum(grad_own * padded_all[:, a:a + row_count, d:d + col_count, :], ax...  81.9 us
    convert_element_type x1, other arithmetic, shards(): return (loss, input_grad.astype(jnp.bfloat16), kernel_grad, text_grad)  74.5 us
    psum x1, blocking collectives, shards(): pooled = lax.psum(pool_part, 'space') / pixel_count  74.3 us
    reduce_sum x1, other arithmetic, normalize(): centre_value = jnp.mean(values, axis=-1, keepdims=True)  72.8 us
    another operation x56, local copies, waits for them, and re-layouts, shards(): jnp.stack([jnp.sum(grad_own * padded_all[:, a:a + row_count, d:d + col_co...  59.6 us
    reduce_sum x1, other arithmetic, shards(): jnp.sum(lax.all_gather(kernel_part, ('dp', 'space')), axis=0) / pixel_count  27.1 us
    all_gather x1, blocking collectives, shards(): lax.all_gather(unit_txt, 'dp', axis=0, tiled=True)  22.4 us
  transfers between devices with their start and end apart: 5, of which 3 were waited for; matrix products, arithmetic and copies ran while one was open for 9% of the time, Pallas kernels for 0%

profile of v1, /device:TPU:1, one launch (start us, length us, event | category | flops | bytes accessed | tf_op | source)
XLA Modules:
  0.0 964.0 jit_solution(6942987264683233123)
XLA Ops:
  7.2 2.5 fusion.104
  9.7 5.1 collective-permute-start.1
  14.8 1.9 collective-permute-start
  17.7 1.3 multiply_reduce_fusion.53
  22.3 22.4 %all-gather.2 = f32[8,1,1024]{2,1,0:T(1,128)S(1)} all-gather(f32[1,1,1024]{2,1,0:T(1,128)S(1)} %fusion.113), channel_id=1, replica_groups=mesh['dp'=8,'space'=32] {'dp'}, dimensions={0}, use_global_device_ids=true | all-gather | bytes 36864 | tf_op jit(solution)/shard_map/all_gather | solution.py:64
  47.7 4.6 maximum_convert_fusion
  52.6 72.8 %fusion.102 = (f32[8,64]{1,0:T(8,128)S(1)}, f32[1,8,64,1536]{3,2,1,0:T(8,128)}) fusion(f32[1536]{0:T(1024)} %param.10, f32[1536]{0:T(1024)S(1)} %copy-done.63, f32[1536]{0:T(1024)S(1)} %copy-done.65, f32[1536]{0:T(1024)S(1)} %copy-done.67, f32[1536]{0:T(1024)S(1)} %copy-done.69, f32[1,14,64,1536]{3,2,1,0:T(8,128)} %maximum_convert_fusion, ...), kind=kLoop, calls=%fused_computation.331 | loop fusion | flops 77856256 | bytes 30994432 | tf_op jit(solution)/shard_map/reduce_sum | solution.py:21
  125.4 2.5 multiply_reduce_fusion.50
  128.9 74.3 %psum.14 = f32[1,1536]{1,0:T(1,128)S(1)} all-reduce(f32[1,1536]{1,0:T(1,128)S(1)} %reduce_sum.573), channel_id=1, replica_groups=mesh['dp'=8,'space'=32] {'space'}, use_global_device_ids=true, to_apply=%region_3.4 | all-reduce | flops 1536 | bytes 12288 | tf_op jit(solution)/shard_map/psum | solution.py:56
  203.2 1.3 fusion.67
  205.8 21.9 %all-gather = f32[8192]{0:T(1024)S(1)} all-gather(f32[1024]{0:T(1024)S(1)} %broadcast_divide_fusion.1), channel_id=2, replica_groups=mesh['dp'=8,'space'=32] {'dp'}, dimensions={0}, use_global_device_ids=true | all-gather | bytes 36864 | tf_op jit(solution)/shard_map/all_gather | solution.py:63
  237.2 16.2 %all-reduce.4 = (f32[]{:T(128)}, f32[8]{0:T(128)S(1)}, f32[8]{0:T(128)S(1)}) all-reduce(f32[]{:T(128)} %bitcast.11, f32[8]{0:T(128)S(1)} %dynamic-update-slice, f32[8]{0:T(128)S(1)} %dynamic-update-slice.1), channel_id=1, replica_groups=mesh['dp'=8,'space'=32] {'dp'}, use_global_device_ids=true, to_apply=%region_11.12 | all-reduce | flops 17 | bytes 136 | tf_op jit(solution)/shard_map/psum | solution.py:82
  255.6 2.5 convolution_reduce_fusion
  260.0 30.9 %multiply_reduce_fusion = (f32[1536]{0:T(1024)}, f32[1536]{0:T(1024)}, f32[1536]{0:T(1024)}, f32[1536]{0:T(1024)}, f32[1536]{0:T(1024)}, /*index=5*/f32[1536]{0:...) fusion(f32[1,14,64,1536]{3,2,1,0:T(8,128)} %maximum_convert_fus, ...), kind=kLoop, calls=%fused_computation.157 | loop fusion | flops 32216064 | bytes 21356544 | tf_op jit(solution)/shard_map/reduce_sum | solution.py:130
  290.9 22.9 %multiply_reduce_fusion.36 = (f32[1536]{0:T(1024)}, f32[1536]{0:T(1024)}, f32[1536]{0:T(1024)}, f32[1536]{0:T(1024)}, f32[1536]{0:T(1024)}, /*index=5*/f32[1536]...) fusion(f32[1,8,64,1536]{3,2,1,0:T(8,128)S(1)} %get-tuple-elemen, ...), kind=kLoop, calls=%fused_computation.193 | loop fusion | flops 20427264 | bytes 15022080 | tf_op jit(solution)/shard_map/reduce_sum | solution.py:130
  313.8 28.1 %multiply_reduce_fusion.1 = (f32[1536]{0:T(1024)}, f32[1536]{0:T(1024)}, f32[1536]{0:T(1024)}, f32[1536]{0:T(1024)}, f32[1536]{0:T(1024)}, /*index=5*/f32[1536]{...) fusion(f32[1,8,64,1536]{3,2,1,0:T(8,128)S(1)} %get-tuple-elemen, ...), kind=kLoop, calls=%fused_computation.158 | loop fusion | flops 28283904 | bytes 15052800 | tf_op jit(solution)/shard_map/reduce_sum | solution.py:130
  347.2 1.3 stack.205
  349.8 1.3 stack.207
  356.3 1.3 stack.214
  357.6 1.3 stack.215
  361.5 1.3 stack.220
  362.8 1.3 stack.221
  370.5 1.3 stack.229
  402.3 3.3 fusion.103
  405.6 12.2 %collective-permute-start.3 = (f32[1,3,64,1536]{3,2,1,0:T(8,128)}, f32[1,3,64,1536]{3,2,1,0:T(8,128)}, u32[]{:S(2)}, u32[]{:S(2)}) collective-permute-start(f32[1,3,64,1536]{3,2,1,0:T(8,128)} %get-tuple-element.113), channel_id=1, source_target_pairs={{1,0},{2,1},{3,2},{4,3},{5,4},{6,5},{7,6},{8,7},{9,8},{10,9},{11,1... | collective-permute-start | bytes 3538952 | tf_op jit(solution)/shard_map/ppermute | solution.py:15
  417.8 2.1 collective-permute-start.2
  422.6 16.2 %collective-permute-done.3 = f32[1,3,64,1536]{3,2,1,0:T(8,128)} collective-permute-done((f32[1,3,64,1536]{3,2,1,0:T(8,128)}, f32[1,3,64,1536]{3,2,1,0:T(8,128)}, u32[]{:S(2)}, u32[]{:S(2)}) %collective-permute-start.3) | collective-permute-done | bytes 1179680 | tf_op jit(solution)/shard_map/ppermute | solution.py:15
  438.8 12.1 %collective-permute-done.2 = f32[1,3,64,1536]{3,2,1,0:T(8,128)} collective-permute-done((f32[1,3,64,1536]{3,2,1,0:T(8,128)}, f32[1,3,64,1536]{3,2,1,0:T(8,128)}, u32[]{:S(2)}, u32[]{:S(2)}) %collective-permute-start.2) | collective-permute-done | bytes 1179680 | tf_op jit(solution)/shard_map/ppermute | solution.py:12
  450.9 5.0 select_maximum_fusion
  456.3 74.5 %fusion.59 = bf16[1,8,64,1536]{3,2,1,0:T(8,128)(2,1)} fusion(f32[1,14,70,1536]{3,2,1,0:T(8,128)} %select_maximum_fusion, f32[1,8,64,1536]{3,2,1,0:T(8,128)} %copy-done.1, f32[1,3,64,1536]{3,2,1,0:T(8,128)} %collective-permute-done.2, f32[1,3,64,1536]{3,2,1,0:T(8,128)} %collective-permute-done.3, f32[1536]{0:T(1024)S(1)} %copy-done.64, ...), kind=kLoop, calls=%fused_computation.211 | loop fusion | flops 81788928 | bytes 139499520 | tf_op jit(solution)/shard_map/convert_element_type | solution.py:141
  530.7 397.5 %all-gather.5.cloned.1.call-done = f32[1792,7,1536]{2,1,0:T(8,128)} async-done(((f32[7,7,1536]{2,1,0:T(8,128)}), f32[1792,7,1536]{2,1,0:T(8,128)}) %all-gather.5.cloned.1.call-update) | async-done | bytes 77070352 | tf_op jit(solution)/shard_map/all_gather | solution.py:140
  928.2 27.1 %reduce_sum.632 = f32[7,7,1536]{2,1,0:T(8,128)S(1)} reduce(f32[256,7,7,1536]{3,2,1,0:T(8,128)} %bitcast.23, f32[]{:T(128)} %constant.12.clone.1), dimensions={0}, to_apply=%region_64.65 | reduce | flops 19192320 | bytes 77371392 | tf_op jit(solution)/shard_map/reduce_sum | solution.py:140
  (274 shorter events, 70.1 us)
Async XLA Ops:
  7.2 196.0 %copy-start = (bf16[1536,1024]{1,0:T(8,128)(2,1)S(1)}, bf16[1536,1024]{1,0:T(8,128)(2,1)}, u32[]{:S(2)}) copy-start(bf16[1536,1024]{1,0:T(8,128)(2,1)} %param.13) | copy-start | bytes 9437188
  7.2 921.0 %all-gather.5.cloned.1.call-start = ((), (), s32[]{:S(2)}) async-start(), calls=%async_computation | async-start | bytes 88424448 | tf_op jit(solution)/shard_map/all_gather | solution.py:140
  9.7 37.9 %collective-permute-start.1 = (bf16[1,3,64,1536]{3,2,1,0:T(8,128)(2,1)}, bf16[1,3,64,1536]{3,2,1,0:T(8,128)(2,1)}, u32[]{:S(2)}, u32[]{:S(2)}) collective-permute-start(bf16[1,3,64,1536]{3,2,1,0:T(8,128)(2,1)} %get-tuple-element.115), channel_id=1, source_target_pairs={{1,0},{2,1},{3,2},{4,3},{5,4},{6,5},{7,6},{8,7},{9,8},{10,9},{11,1... | collective-permute-start | bytes 1769480 | tf_op jit(solution)/shard_map/ppermute | solution.py:15
  14.8 32.8 %collective-permute-start = (bf16[1,3,64,1536]{3,2,1,0:T(8,128)(2,1)}, bf16[1,3,64,1536]{3,2,1,0:T(8,128)(2,1)}, u32[]{:S(2)}, u32[]{:S(2)}) collective-permute-start(bf16[1,3,64,1536]{3,2,1,0:T(8,128)(2,1)} %get-tuple-element.114), channel_id=1, source_target_pairs={{0,1},{1,2},{2,3},{3,4},{4,5},{5,6},{6,7},{7,8},{8,9},{9,10},{10,1... | collective-permute-start | bytes 1769480 | tf_op jit(solution)/shard_map/ppermute | solution.py:12
  128.2 102.9 %copy-start.86 = (f32[1,1024]{1,0:T(1,128)S(1)}, f32[1,1024]{1,0:T(1,128)}, u32[]{:S(2)}) copy-start(f32[1,1024]{1,0:T(1,128)} %param.14) | copy-start | bytes 12292
  405.6 33.2 %collective-permute-start.3 = (f32[1,3,64,1536]{3,2,1,0:T(8,128)}, f32[1,3,64,1536]{3,2,1,0:T(8,128)}, u32[]{:S(2)}, u32[]{:S(2)}) collective-permute-start(f32[1,3,64,1536]{3,2,1,0:T(8,128)} %get-tuple-element.113), channel_id=1, source_target_pairs={{1,0},{2,1},{3,2},{4,3},{5,4},{6,5},{7,6},{8,7},{9,8},{10,9},{11,1... | collective-permute-start | bytes 3538952 | tf_op jit(solution)/shard_map/ppermute | solution.py:15
  417.8 33.1 %collective-permute-start.2 = (f32[1,3,64,1536]{3,2,1,0:T(8,128)}, f32[1,3,64,1536]{3,2,1,0:T(8,128)}, u32[]{:S(2)}, u32[]{:S(2)}) collective-permute-start(f32[1,3,64,1536]{3,2,1,0:T(8,128)} %get-tuple-element.112), channel_id=1, source_target_pairs={{0,1},{1,2},{2,3},{3,4},{4,5},{5,6},{6,7},{7,8},{8,9},{9,10},{10,1... | collective-permute-start | bytes 3538952 | tf_op jit(solution)/shard_map/ppermute | solution.py:12
  422.3 33.6 %copy-start.14 = (f32[1536]{0:T(1024)S(1)}, f32[1536]{0:T(1024)}, u32[]{:S(2)}) copy-start(f32[1536]{0:T(1024)} %get-tuple-element.97) | copy-start | bytes 18436
  422.3 33.6 %copy-start.16 = (f32[1536]{0:T(1024)S(1)}, f32[1536]{0:T(1024)}, u32[]{:S(2)}) copy-start(f32[1536]{0:T(1024)} %get-tuple-element.98) | copy-start | bytes 18436
  422.3 33.6 %copy-start.18 = (f32[1536]{0:T(1024)S(1)}, f32[1536]{0:T(1024)}, u32[]{:S(2)}) copy-start(f32[1536]{0:T(1024)} %get-tuple-element.99) | copy-start | bytes 18436
  422.3 33.6 %copy-start.20 = (f32[1536]{0:T(1024)S(1)}, f32[1536]{0:T(1024)}, u32[]{:S(2)}) copy-start(f32[1536]{0:T(1024)} %get-tuple-element.100) | copy-start | bytes 18436
  422.3 33.6 %copy-start.22 = (f32[1536]{0:T(1024)S(1)}, f32[1536]{0:T(1024)}, u32[]{:S(2)}) copy-start(f32[1536]{0:T(1024)} %get-tuple-element.101) | copy-start | bytes 18436
  422.3 33.6 %copy-start.24 = (f32[1536]{0:T(1024)S(1)}, f32[1536]{0:T(1024)}, u32[]{:S(2)}) copy-start(f32[1536]{0:T(1024)} %get-tuple-element.72) | copy-start | bytes 18436
  422.3 33.6 %copy-start.26 = (f32[1536]{0:T(1024)S(1)}, f32[1536]{0:T(1024)}, u32[]{:S(2)}) copy-start(f32[1536]{0:T(1024)} %get-tuple-element.73) | copy-start | bytes 18436
  422.3 33.6 %copy-start.28 = (f32[1536]{0:T(1024)S(1)}, f32[1536]{0:T(1024)}, u32[]{:S(2)}) copy-start(f32[1536]{0:T(1024)} %get-tuple-element.74) | copy-start | bytes 18436
  422.3 33.6 %copy-start.30 = (f32[1536]{0:T(1024)S(1)}, f32[1536]{0:T(1024)}, u32[]{:S(2)}) copy-start(f32[1536]{0:T(1024)} %get-tuple-element.75) | copy-start | bytes 18436
  422.4 33.6 %copy-start.32 = (f32[1536]{0:T(1024)S(1)}, f32[1536]{0:T(1024)}, u32[]{:S(2)}) copy-start(f32[1536]{0:T(1024)} %get-tuple-element.76) | copy-start | bytes 18436
  422.4 33.6 %copy-start.34 = (f32[1536]{0:T(1024)S(1)}, f32[1536]{0:T(1024)}, u32[]{:S(2)}) copy-start(f32[1536]{0:T(1024)} %get-tuple-element.77) | copy-start | bytes 18436
  422.4 33.6 %copy-start.36 = (f32[1536]{0:T(1024)S(1)}, f32[1536]{0:T(1024)}, u32[]{:S(2)}) copy-start(f32[1536]{0:T(1024)} %get-tuple-element.78) | copy-start | bytes 18436
  422.4 33.6 %copy-start.38 = (f32[1536]{0:T(1024)S(1)}, f32[1536]{0:T(1024)}, u32[]{:S(2)}) copy-start(f32[1536]{0:T(1024)} %get-tuple-element.79) | copy-start | bytes 18436
  422.4 33.6 %copy-start.40 = (f32[1536]{0:T(1024)S(1)}, f32[1536]{0:T(1024)}, u32[]{:S(2)}) copy-start(f32[1536]{0:T(1024)} %get-tuple-element.80) | copy-start | bytes 18436
  422.4 33.6 %copy-start.42 = (f32[1536]{0:T(1024)S(1)}, f32[1536]{0:T(1024)}, u32[]{:S(2)}) copy-start(f32[1536]{0:T(1024)} %get-tuple-element.81) | copy-start | bytes 18436
  422.4 33.6 %copy-start.44 = (f32[1536]{0:T(1024)S(1)}, f32[1536]{0:T(1024)}, u32[]{:S(2)}) copy-start(f32[1536]{0:T(1024)} %get-tuple-element.82) | copy-start | bytes 18436
  422.4 33.6 %copy-start.46 = (f32[1536]{0:T(1024)S(1)}, f32[1536]{0:T(1024)}, u32[]{:S(2)}) copy-start(f32[1536]{0:T(1024)} %get-tuple-element.83) | copy-start | bytes 18436
  422.4 33.6 %copy-start.48 = (f32[1536]{0:T(1024)S(1)}, f32[1536]{0:T(1024)}, u32[]{:S(2)}) copy-start(f32[1536]{0:T(1024)} %get-tuple-element.84) | copy-start | bytes 18436
  422.4 33.6 %copy-start.50 = (f32[1536]{0:T(1024)S(1)}, f32[1536]{0:T(1024)}, u32[]{:S(2)}) copy-start(f32[1536]{0:T(1024)} %get-tuple-element.85) | copy-start | bytes 18436
  422.5 33.6 %copy-start.52 = (f32[1536]{0:T(1024)S(1)}, f32[1536]{0:T(1024)}, u32[]{:S(2)}) copy-start(f32[1536]{0:T(1024)} %get-tuple-element.86) | copy-start | bytes 18436
  422.5 33.6 %copy-start.54 = (f32[1536]{0:T(1024)S(1)}, f32[1536]{0:T(1024)}, u32[]{:S(2)}) copy-start(f32[1536]{0:T(1024)} %get-tuple-element.87) | copy-start | bytes 18436
  422.5 33.6 %copy-start.56 = (f32[1536]{0:T(1024)S(1)}, f32[1536]{0:T(1024)}, u32[]{:S(2)}) copy-start(f32[1536]{0:T(1024)} %get-tuple-element.88) | copy-start | bytes 18436
  422.5 33.6 %copy-start.58 = (f32[1536]{0:T(1024)S(1)}, f32[1536]{0:T(1024)}, u32[]{:S(2)}) copy-start(f32[1536]{0:T(1024)} %get-tuple-element.89) | copy-start | bytes 18436
  422.5 33.6 %copy-start.60 = (f32[1536]{0:T(1024)S(1)}, f32[1536]{0:T(1024)}, u32[]{:S(2)}) copy-start(f32[1536]{0:T(1024)} %get-tuple-element.90) | copy-start | bytes 18436
  422.5 33.6 %copy-start.62 = (f32[1536]{0:T(1024)S(1)}, f32[1536]{0:T(1024)}, u32[]{:S(2)}) copy-start(f32[1536]{0:T(1024)} %get-tuple-element.53) | copy-start | bytes 18436
  (64 other events, 787.5 us)
Sparse Core Ops, SparseCore 0:
  402.5 525.7 all-gather.4
